TPU v7x, 32 devices: a whole 2x2x4 slice. The times are simulated.
32 devices in a mesh: uv: 8 (over y, x, core), chan: 4 (over z).
Axes of the slice: x: 2, y: 2, z: 4, core: 2. Of those that a mesh axis runs over, the one named last changes fastest.
Arguments:
- vis: bfloat16 [98304, 2, 1024], P('uv', None, 'chan'), may hold values from -6 to 6
- row_cell: int32 [98304], P('uv'), may hold values from 0 to 127
- tap_weight: bfloat16 [8, 98304], P(None, 'uv'), may hold values from 0.029907227 to 0.29882812
- tap_offset: int32 [8], replicated, may hold values from -32 to 32
- block_tile: int32 [768], P('uv'), may hold values from 0 to 79, as said below
- tile_owner: int32 [80], replicated, may hold values from 0 to 7, as said below
- galaxy: bfloat16 [152, 128, 2048], P('uv', 'chan'), may hold values from -6 to 6
Outputs:
- delay_cube: bfloat16 [152, 128, 2048], P('uv', 'chan')
- cross_power: float32 [152, 1024], P('uv')
Inputs may be any that keep to these rules, and one draw needn't show every extreme that they name: `tile_owner`: each of the 8 owners holds 1 to 19 tiles, and some owner exactly 19. `block_tile`: of the 96 row blocks of one index of uv, at most 22 lie in tiles of one owner, and exactly 22 lie in the tiles of some owner.
All inputs are finite; a program needn't handle non-finite values.
Results may differ from a plain program's by a relative error of at most 0.0059.
Values may be sent and summed in bfloat16 or wider, within the bound.
No kernel may reach another device: no remote copies, remote signals or barrier semaphores. Data moves between devices by JAX's collectives and lax.ppermute only.
A program may use at most 128 MiB of HBM per device.

v0:
```python
import math
import jax
import jax.numpy as jnp
from jax import lax
from jax.sharding import PartitionSpec as P

CH = 1024
BR = 128
TC = 128
KT = 8
TILES_DEV = 10


def tile_ranks(tile_owner, owners):
    onehot = (tile_owner[:, None] == jnp.arange(owners, dtype=jnp.int32)[None, :]).astype(jnp.int32)
    before = jnp.cumsum(onehot, axis=0) - onehot
    return jnp.sum(before * onehot, axis=1)


def kernel_matrix(cells, weights, tap_offset):
    positions = jnp.arange(TC, dtype=jnp.int32)
    total = jnp.zeros(cells.shape[:-1] + (TC, cells.shape[-1]), jnp.float32)
    for k in range(KT):
        target = cells + tap_offset[k]
        hit = target[..., None, :] == positions[:, None]
        total = total + jnp.where(
            hit, weights[..., k, :].astype(jnp.float32)[..., None, :], jnp.float32(0.0)
        )
    return total.astype(jnp.bfloat16)


def delay_table():
    freq = jnp.arange(CH, dtype=jnp.int32)
    phase = (freq[:, None] * freq[None, :] % CH).astype(jnp.float32) * jnp.float32(
        2.0 * math.pi / CH
    )
    cosine = jnp.cos(phase)
    sine = jnp.sin(phase)
    x = freq.astype(jnp.float32) * jnp.float32(2.0 * math.pi / CH)
    taper = 0.35875 - 0.48829 * jnp.cos(x) + 0.14128 * jnp.cos(2.0 * x) - 0.01168 * jnp.cos(3.0 * x)
    scale = (taper / jnp.float32(math.sqrt(CH)))[:, None]
    upper = jnp.concatenate([cosine * scale, -sine * scale], axis=1)
    lower = jnp.concatenate([sine * scale, cosine * scale], axis=1)
    return jnp.concatenate([upper, lower], axis=0).astype(jnp.bfloat16)


def body(vis, row_cell, tap_weight, tap_offset, block_tile, tile_owner, galaxy):
    n_owners = lax.axis_size("uv")
    nblocks = block_tile.shape[0]
    mean_load = nblocks // n_owners
    capacity = mean_load + (TILES_DEV - 1) * mean_load // TILES_DEV
    slots_dev = 2 * TILES_DEV - 1
    chan_dev = vis.shape[2]
    buffer_size = n_owners * capacity
    rank_of_tile = tile_ranks(tile_owner, n_owners)
    target_owner = tile_owner[block_tile]
    owner_hot = (target_owner[:, None] == jnp.arange(n_owners, dtype=jnp.int32)[None, :]).astype(
        jnp.int32
    )
    earlier = jnp.cumsum(owner_hot, axis=0) - owner_hot
    place = target_owner * capacity + jnp.sum(earlier * owner_hot, axis=1)
    blocks = vis.reshape(nblocks, BR, 2 * chan_dev)
    cells = row_cell.reshape(nblocks, BR)
    weights = jnp.transpose(tap_weight.reshape(KT, nblocks, BR), (1, 0, 2))
    sent_vis = jnp.zeros((buffer_size, BR, 2 * chan_dev), jnp.bfloat16).at[place].set(blocks)
    sent_tile = jnp.full((buffer_size,), -1, jnp.int32).at[place].set(block_tile)
    sent_cells = jnp.zeros((buffer_size, BR), jnp.int32).at[place].set(cells)
    sent_weights = jnp.zeros((buffer_size, KT, BR), jnp.bfloat16).at[place].set(weights)
    got_vis, got_tile, got_cells, got_weights = (
        lax.all_to_all(sent_vis, "uv", split_axis=0, concat_axis=0, tiled=True),
        lax.all_to_all(sent_tile, "uv", split_axis=0, concat_axis=0, tiled=True),
        lax.all_to_all(sent_cells, "uv", split_axis=0, concat_axis=0, tiled=True),
        lax.all_to_all(sent_weights, "uv", split_axis=0, concat_axis=0, tiled=True),
    )
    got_matrix = kernel_matrix(got_cells, got_weights, tap_offset)
    contrib = jnp.einsum("bcr,brf->bcf", got_matrix, got_vis, preferred_element_type=jnp.float32)
    slot = jnp.where(got_tile >= 0, rank_of_tile[jnp.maximum(got_tile, 0)], -1)
    pick = (slot[:, None] == jnp.arange(slots_dev, dtype=jnp.int32)[None, :]).astype(jnp.float32)
    grid = jnp.einsum("bs,bcf->scf", pick, contrib, precision=lax.Precision.HIGHEST)
    gridded = grid.astype(jnp.bfloat16).reshape(slots_dev, TC, 2, chan_dev)
    table = delay_table()
    piece = lax.all_to_all(gridded, "chan", split_axis=1, concat_axis=3, tiled=True)
    count = piece.shape[0]
    cells_part = piece.shape[1]
    flat = piece.reshape(count * cells_part, 2 * CH)
    out = jnp.dot(flat, table, preferred_element_type=jnp.float32)
    delay = out.reshape(count, cells_part, 2 * CH)
    galaxy_f = galaxy.astype(jnp.float32)
    product = delay[..., :CH] * galaxy_f[..., :CH] + delay[..., CH:] * galaxy_f[..., CH:]
    local_power = jnp.sum(product, axis=1)
    power = lax.psum(local_power, "chan") / jnp.float32(math.sqrt(TC))
    return (delay.astype(jnp.bfloat16), power)


def solution(mesh):
    return jax.shard_map(
        body,
        mesh=mesh,
        in_specs=(
            P("uv", None, "chan"),
            P("uv"),
            P(None, "uv"),
            P(),
            P("uv"),
            P(),
            P("uv", "chan", None),
        ),
        out_specs=(P("uv", "chan", None), P("uv", None)),
        check_vma=False,
    )
```

profile of v0, /device:TPU:0, one launch (start us, length us, event | category | flops | bytes accessed | tf_op | source)
XLA Modules:
  0.0 569.6 jit_solution(16998166635543470072)
XLA Ops:
  7.2 0.0 copy-start
  7.2 0.7 compare_select_fusion.1
  7.9 1.6 gather_fusion
  9.4 0.1 fusion.41
  9.5 0.1 reduce_window_sum.22
  9.7 0.2 select_reduce_fusion
  9.9 1.0 scatter_custom_fusion
  10.9 0.7 all_to_all.29
  11.6 5.2 all-to-all-start
  16.8 0.8 scatter_custom_fusion.1
  17.6 0.6 all_to_all.31
  18.2 3.1 all-to-all-done
  21.4 3.4 all-to-all-start.1
  24.7 0.8 broadcast_in_dim.144
  25.5 10.6 %scatter_fusion = bf16[176,8,128]{2,1,0:T(8,128)(2,1)} fusion(bf16[176,8,128]{2,1,0:T(8,128)(2,1)} %broadcast_in_dim.144, s32[96]{0:T(128)S(1)} %fusion.47, bf16[96,8,128]{2,1,0:T(8,128)(2,1)} %bitcast.45), kind=kCustom, calls=%fused_computation.4 | custom fusion | bytes 590208 | tf_op jit(solution)/shard_map/scatter | solution.py:68
  36.1 4.1 all-to-all-start.2
  40.3 20.5 %reshape.204 = bf16[96,128,512]{2,1,0:T(8,128)(2,1)} reshape(bf16[12288,2,256]{2,1,0:T(2,128)(2,1)} %param.7) | data formatting | bytes 25165824 | tf_op jit(solution)/shard_map/reshape | solution.py:62
  60.7 7.9 %broadcast_in_dim.170 = bf16[176,128,512]{2,1,0:T(8,128)(2,1)} broadcast(bf16[]{:T(256)} %constant.24.clone.1), dimensions={} | broadcast | bytes 23068674 | tf_op jit(solution)/shard_map/broadcast_in_dim | solution.py:65
  68.6 33.0 %scatter_fusion.1 = bf16[176,128,512]{2,1,0:T(8,128)(2,1)} fusion(bf16[176,128,512]{2,1,0:T(8,128)(2,1)} %broadcast_in_dim.170, s32[96]{0:T(128)S(1)} %fusion.47, bf16[96,128,512]{2,1,0:T(8,128)(2,1)} %reshape.204), kind=kCustom, calls=%fused_computation.5 | custom fusion | bytes 37749120 | tf_op jit(solution)/shard_map/scatter | solution.py:65
  101.6 6.4 %all-to-all-start.3 = ((bf16[176,128,512]{2,1,0:T(8,128)(2,1)}), bf16[176,128,512]{2,1,0:T(8,128)(2,1)}, u32[]{:S(2)}, u32[]{:S(2)}) async-start(bf16[176,128,512]{2,1,0:T(8,128)(2,1)} %scatter_fusion.1), calls=%async_computation.3 | async-start | bytes 46137344 | tf_op jit(solution)/shard_map/all_to_all | solution.py:70
  108.1 0.1 fusion.43
  108.1 0.1 reduce_window_sum.23
  108.3 0.7 fusion.52
  108.9 0.2 select_reduce_fusion.1
  109.1 0.1 reshape.170
  109.2 0.1 ge.11
  109.3 1.6 gather_fusion.1
  110.9 5.1 broadcast_add_fusion.7
  116.2 0.5 slice_convert_fusion.7
  116.6 242.7 %all-to-all-done.3 = bf16[176,128,512]{2,1,0:T(8,128)(2,1)} async-done(((bf16[176,128,512]{2,1,0:T(8,128)(2,1)}), bf16[176,128,512]{2,1,0:T(8,128)(2,1)}, u32[]{:S(2)}, u32[]{:S(2)}) %all-to-all-start.3) | async-done | bytes 23068704 | tf_op jit(solution)/shard_map/all_to_all | solution.py:70
  359.4 29.0 %fusion.9 = f32[176,128,512]{2,1,0:T(8,128)} fusion(bf16[176,128,512]{2,1,0:T(8,128)(2,1)} %all-to-all-done.3, f32[176,128]{1,0:T(8,128)S(1)} %bitcast.47, s32[176,128]{1,0:T(8,128)S(1)} %add.223, f32[176,128]{1,0:T(8,128)S(1)} %bitcast.48, s32[176,128]{1,0:T(8,128)S(1)} %add.219, f32[176,128]{1,0:T(8,128)S(1)} %bitcast.49, s32[176,128]{1,0:T(8,128)S(1)} %add.215, ...), kind=kOutput, calls=%fused_computation.28 | convolution fusion | flops 3021996032 | bytes 70647808 | tf_op jit(solution)/shard_map/bcr,brf->bcf/dot_general | solution.py:76
  388.4 49.7 %fusion.35 = bf16[19,128,512]{2,0,1:T(8,128)(2,1)S(1)} fusion(f32[176,128,512]{2,1,0:T(8,128)} %fusion.9, s32[176]{0:T(256)S(1)} %broadcast_select_fusion), kind=kOutput, calls=%fused_computation.59 | convolution fusion | flops 2631077120 | bytes 48628416 | tf_op jit(solution)/shard_map/bs,bcf->scf/dot_general | solution.py:79
  438.1 3.4 copy.18
  441.5 7.4 %copy.19 = bf16[19,128,2,256]{3,2,0,1:T(2,128)(2,1)} copy(bf16[19,128,2,256]{1,3,2,0:T(8,128)(2,1)} %bitcast.43) | data formatting | bytes 4980736 | tf_op jit(solution)/shard_map/reshape | solution.py:80
  448.9 4.9 all-to-all-start.4
  453.8 4.6 convert_element_type.65
  458.3 0.1 subtract_multiply_fusion
  458.4 19.1 %multiply_convert_fusion.1 = (bf16[1024,1024]{1,0:T(8,128)(2,1)}, bf16[1024,1024]{1,0:T(8,128)(2,1)}, bf16[1024,1024]{1,0:T(8,128)(2,1)}) fusion(f32[1024]{0:T(1024)S(1)} %subtract_multiply_fusion), kind=kLoop, calls=%fused_computation.50 | loop fusion | flops 22020096 | bytes 6295552 | tf_op jit(solution)/shard_map/convert.13
  477.5 30.1 %all-to-all-done.4 = bf16[19,128,2,256]{3,2,0,1:T(2,128)(2,1)S(1)} async-done(((bf16[19,128,2,256]{3,2,0,1:T(2,128)(2,1)}), bf16[19,128,2,256]{3,2,0,1:T(2,128)(2,1)S(1)}, u32[]{:S(2)}, u32[]{:S(2)}) %all-to-all-start.4) | async-done | bytes 2490400 | tf_op jit(solution)/shard_map/all_to_all | solution.py:82
  507.6 0.4 copy.20
  508.1 2.2 copy.21
  510.2 0.0 slice-start
  510.2 3.0 dot_general.13
  513.3 11.1 %fusion.53 = (bf16[19,32,2048]{2,1,0:T(8,128)(2,1)}, f32[19,32,2048]{2,1,0:T(8,128)S(1)}) fusion(bf16[19,32,2048]{2,1,0:T(8,128)(2,1)} %dot_general.13, bf16[1024,1024]{1,0:T(8,128)(2,1)} %get-tuple-element.20, bf16[1024,1024]{1,0:T(8,128)(2,1)} %get-tuple-element.19, bf16[1024,1024]{1,0:T(8,128)(2,1)} %get-tuple-element.18), kind=kOutput, calls=%fused_computation.104 | convolution fusion | flops 5135073280 | bytes 16252928 | tf_op jit(solution)/shard_map/dot_general | solution.py:86
  524.3 2.0 fusion.34
  526.3 0.0 all-reduce.2.cloned.1.call-update
  526.4 34.8 %all-reduce.2.cloned.1.call-done = f32[19,1024]{1,0:T(8,128)} async-done(((f32[19,1024]{1,0:T(8,128)}), f32[19,1024]{1,0:T(8,128)}) %all-reduce.2.cloned.1.call-update) | async-done | bytes 77840 | tf_op jit(solution)/shard_map/psum | solution.py:91
  561.2 1.5 broadcast_multiply_fusion
  (28 shorter events, 0.2 us)
Async XLA Ops:
  7.2 9.6 %copy-start = (s32[12288]{0:T(1024)S(1)}, s32[12288]{0:T(1024)}, u32[]{:S(2)}) copy-start(s32[12288]{0:T(1024)} %param.8) | copy-start | bytes 147460
  11.6 9.8 %all-to-all-start = ((s32[8,22,1]{1,2,0:T(1,128)}), s32[8,22,1]{1,2,0:T(1,128)S(1)}, u32[]{:S(2)}, u32[]{:S(2)}) async-start(s32[8,22,1]{1,2,0:T(1,128)} %bitcast.2), calls=%async_computation | async-start | bytes 8192 | tf_op jit(solution)/shard_map/all_to_all | solution.py:71
  21.4 14.8 %all-to-all-start.1 = ((s32[8,22,128]{2,1,0:T(8,128)}), s32[8,22,128]{2,1,0:T(8,128)S(1)}, u32[]{:S(2)}, u32[]{:S(2)}) async-start(s32[8,22,128]{2,1,0:T(8,128)} %all_to_all.31), calls=%async_computation.1 | async-start | bytes 196608 | tf_op jit(solution)/shard_map/all_to_all | solution.py:72
  36.1 65.5 %all-to-all-start.2 = ((bf16[176,8,128]{2,1,0:T(8,128)(2,1)}), bf16[176,8,128]{2,1,0:T(8,128)(2,1)S(1)}, u32[]{:S(2)}, u32[]{:S(2)}) async-start(bf16[176,8,128]{2,1,0:T(8,128)(2,1)} %scatter_fusion), calls=%async_computation.2 | async-start | bytes 720896 | tf_op jit(solution)/shard_map/all_to_all | solution.py:73
  101.6 6.5 %copy-start.2 = (s32[80]{0:T(128)S(1)}, s32[80]{0:T(128)}, u32[]{:S(2)}) copy-start(s32[80]{0:T(128)} %param.12) | copy-start | bytes 964
  101.6 6.7 %copy-start.3 = (s32[8]{0:T(128)S(1)}, s32[8]{0:T(128)}, u32[]{:S(2)}) copy-start(s32[8]{0:T(128)} %param.10) | copy-start | bytes 100
  101.6 257.8 %all-to-all-start.3 = ((bf16[176,128,512]{2,1,0:T(8,128)(2,1)}), bf16[176,128,512]{2,1,0:T(8,128)(2,1)}, u32[]{:S(2)}, u32[]{:S(2)}) async-start(bf16[176,128,512]{2,1,0:T(8,128)(2,1)} %scatter_fusion.1), calls=%async_computation.3 | async-start | bytes 46137344 | tf_op jit(solution)/shard_map/all_to_all | solution.py:70
  448.9 58.7 %all-to-all-start.4 = ((bf16[19,128,2,256]{3,2,0,1:T(2,128)(2,1)}), bf16[19,128,2,256]{3,2,0,1:T(2,128)(2,1)S(1)}, u32[]{:S(2)}, u32[]{:S(2)}) async-start(bf16[19,128,2,256]{3,2,0,1:T(2,128)(2,1)} %copy.19), calls=%async_computation.4 | async-start | bytes 4980736 | tf_op jit(solution)/shard_map/all_to_all | solution.py:82
  453.8 107.4 %all-reduce.2.cloned.1.call-start = ((), (), s32[]{:S(2)}) async-start(), calls=%async_computation.5 | async-start | bytes 196608 | tf_op jit(solution)/shard_map/psum | solution.py:91
  510.2 14.1 %slice-start = ((s8[4980736]{0:T(1024)(128)(4,1)}), s8[786432]{0:T(1024)(128)(4,1)S(1)}, s32[]{:S(2)}) async-start(s8[4980736]{0:T(1024)(128)(4,1)} %bitcast.41), calls=%async_computation.6 | async-start | bytes 1572864
  513.3 11.1 %slice-start.1 = ((s8[4980736]{0:T(1024)(128)(4,1)}), s8[4194304]{0:T(1024)(128)(4,1)S(1)}, s32[]{:S(2)}) async-start(s8[4980736]{0:T(1024)(128)(4,1)} %bitcast.41), calls=%async_computation.7 | async-start | bytes 8388608
  513.3 49.4 %copy-start.1 = (s32[12288]{0:T(1024)S(1)}, s32[12288]{0:T(1024)}, u32[]{:S(2)}) copy-start(s32[12288]{0:T(1024)} %param.8) | copy-start | bytes 147460
Sparse Core Ops, SparseCore 0:
  526.5 34.6 all-reduce.1
where the time goes:
time: 572 us; the launch traced here: 570 us
  waiting for transfers between devices  311 us (54%)
  local copies, waits for them, and re-layouts  96.4 us (17%)
  matrix products  89.8 us (16%)
  other arithmetic  34.3 us (6%)
  starting transfers between devices  24 us (4%)
  between operations  14.3 us (2%)
    all_to_all x1, waiting for transfers between devices, body(): lax.all_to_all(sent_vis, 'uv', split_axis=0, concat_axis=0, tiled=True)  243 us
    dot_general x1, matrix products, body(): jnp.einsum('bs,bcf->scf', pick, contrib, precision=lax.Precision.HIGHEST)  49.7 us
    psum x1, waiting for transfers between devices, body(): power = lax.psum(local_power, 'chan') / jnp.float32(math.sqrt(TC))  34.8 us
    scatter x1, local copies, waits for them, and re-layouts, body(): jnp.zeros((buffer_size, BR, 2 * chan_dev), jnp.bfloat16).at[place]  33 us
    all_to_all x1, waiting for transfers between devices, body(): lax.all_to_all(gridded, 'chan', split_axis=1, concat_axis=3, tiled=True)  30.1 us
    dot_general x1, matrix products, body(): jnp.einsum('bcr,brf->bcf', got_matrix, got_vis, preferred_element_type=jn...  29 us
    reshape x1, local copies, waits for them, and re-layouts, body(): blocks = vis.reshape(nblocks, BR, 2 * chan_dev)  20.5 us
    another operation x1, other arithmetic  19.1 us
  transfers between devices with their start and end apart: 6, of which 4 were waited for; matrix products, arithmetic and copies ran while one was open for 19% of the time, Pallas kernels for 0%

commit v1 on v0

--- a/solution.py
+++ b/solution.py
@@ -79,7 +79,10 @@
     grid = jnp.einsum("bs,bcf->scf", pick, contrib, precision=lax.Precision.HIGHEST)
     gridded = grid.astype(jnp.bfloat16).reshape(slots_dev, TC, 2, chan_dev)
     table = delay_table()
-    piece = lax.all_to_all(gridded, "chan", split_axis=1, concat_axis=3, tiled=True)
+    piece = jnp.concatenate(
+        lax.all_to_all(jnp.stack(jnp.split(gridded, lax.axis_size("chan"), axis=1)), "chan", 0, 0),
+        axis=3,
+    )
     count = piece.shape[0]
     cells_part = piece.shape[1]
     flat = piece.reshape(count * cells_part, 2 * CH)

time: 572 us -> 585 us (1.023)
  local copies, waits for them, and re-layouts: 96.4 us -> 106 us
    another operation x0 -> x5, local copies, waits for them, and re-layouts: none -> 14.7 us  [body(): jnp.stack(jnp.split(gridded, lax.axis_size('chan'), axis=1))]
    another operation x1 -> x2, other arithmetic: 19.1 us -> 22.3 us
  transfers between devices with their start and end apart: 6 -> 6, of which waited for: 4 -> 4; matrix products, arithmetic and copies ran while one was open for 19% -> 18% of each run, Pallas kernels for 0% -> 0%
where the time goes in v1:
time: 585 us; the launch traced here: 583 us
  waiting for transfers between devices  311 us (53%)
  local copies, waits for them, and re-layouts  106 us (18%)
  matrix products  89.9 us (15%)
  other arithmetic  37.5 us (6%)
  starting transfers between devices  24 us (4%)
  between operations  14.3 us (2%)
    all_to_all x1, waiting for transfers between devices, body(): lax.all_to_all(sent_vis, 'uv', split_axis=0, concat_axis=0, tiled=True)  243 us
    dot_general x1, matrix products, body(): jnp.einsum('bs,bcf->scf', pick, contrib, precision=lax.Precision.HIGHEST)  50.6 us
    psum x1, waiting for transfers between devices, body(): power = lax.psum(local_power, 'chan') / jnp.float32(math.sqrt(TC))  34.8 us
    scatter x1, local copies, waits for them, and re-layouts, body(): jnp.zeros((buffer_size, BR, 2 * chan_dev), jnp.bfloat16).at[place]  33 us
    all_to_all x1, waiting for transfers between devices, body(): lax.all_to_all(jnp.stack(jnp.split(gridded, lax.axis_size('chan'), axis=1...  30.1 us
    dot_general x1, matrix products, body(): jnp.einsum('bcr,brf->bcf', got_matrix, got_vis, preferred_element_type=jn...  29 us
    reshape x1, local copies, waits for them, and re-layouts, body(): blocks = vis.reshape(nblocks, BR, 2 * chan_dev)  20.5 us
    another operation x1, other arithmetic  19.1 us
  transfers between devices with their start and end apart: 6, of which 4 were waited for; matrix products, arithmetic and copies ran while one was open for 18% of the time, Pallas kernels for 0%

profile of v1, /device:TPU:0, one launch (start us, length us, event | category | flops | bytes accessed | tf_op | source)
XLA Modules:
  0.0 583.0 jit_solution(230414461117738053)
XLA Ops:
  7.2 0.7 compare_select_fusion.1
  7.9 1.6 gather_fusion
  9.4 0.1 fusion.41
  9.5 0.1 reduce_window_sum.22
  9.7 0.2 select_reduce_fusion
  9.9 1.0 scatter_custom_fusion
  10.9 0.7 all_to_all.21
  11.6 5.2 all-to-all-start
  16.8 0.8 scatter_custom_fusion.1
  17.6 0.6 all_to_all.23
  18.2 3.1 all-to-all-done
  21.4 3.4 all-to-all-start.1
  24.7 0.8 broadcast_in_dim.144
  25.5 10.6 %scatter_fusion = bf16[176,8,128]{2,1,0:T(8,128)(2,1)} fusion(bf16[176,8,128]{2,1,0:T(8,128)(2,1)} %broadcast_in_dim.144, s32[96]{0:T(128)S(1)} %fusion.47, bf16[96,8,128]{2,1,0:T(8,128)(2,1)} %bitcast.51), kind=kCustom, calls=%fused_computation.4 | custom fusion | bytes 590208 | tf_op jit(solution)/shard_map/scatter | solution.py:68
  36.1 4.1 all-to-all-start.2
  40.3 20.5 %reshape.206 = bf16[96,128,512]{2,1,0:T(8,128)(2,1)} reshape(bf16[12288,2,256]{2,1,0:T(2,128)(2,1)} %param.7) | data formatting | bytes 25165824 | tf_op jit(solution)/shard_map/reshape | solution.py:62
  60.7 7.9 %broadcast_in_dim.170 = bf16[176,128,512]{2,1,0:T(8,128)(2,1)} broadcast(bf16[]{:T(256)} %constant.24.clone.1), dimensions={} | broadcast | bytes 23068674 | tf_op jit(solution)/shard_map/broadcast_in_dim | solution.py:65
  68.6 33.0 %scatter_fusion.1 = bf16[176,128,512]{2,1,0:T(8,128)(2,1)} fusion(bf16[176,128,512]{2,1,0:T(8,128)(2,1)} %broadcast_in_dim.170, s32[96]{0:T(128)S(1)} %fusion.47, bf16[96,128,512]{2,1,0:T(8,128)(2,1)} %reshape.206), kind=kCustom, calls=%fused_computation.5 | custom fusion | bytes 37749120 | tf_op jit(solution)/shard_map/scatter | solution.py:65
  101.6 6.4 %all-to-all-start.3 = ((bf16[176,128,512]{2,1,0:T(8,128)(2,1)}), bf16[176,128,512]{2,1,0:T(8,128)(2,1)}, u32[]{:S(2)}, u32[]{:S(2)}) async-start(bf16[176,128,512]{2,1,0:T(8,128)(2,1)} %scatter_fusion.1), calls=%async_computation.3 | async-start | bytes 46137344 | tf_op jit(solution)/shard_map/all_to_all | solution.py:70
  108.1 0.1 fusion.43
  108.1 0.1 reduce_window_sum.23
  108.3 0.7 fusion.52
  108.9 0.2 select_reduce_fusion.1
  109.1 0.1 reshape.172
  109.2 0.1 ge.11
  109.3 1.6 gather_fusion.1
  110.9 5.1 broadcast_add_fusion.7
  116.2 0.5 slice_convert_fusion.7
  116.6 242.7 %all-to-all-done.3 = bf16[176,128,512]{2,1,0:T(8,128)(2,1)} async-done(((bf16[176,128,512]{2,1,0:T(8,128)(2,1)}), bf16[176,128,512]{2,1,0:T(8,128)(2,1)}, u32[]{:S(2)}, u32[]{:S(2)}) %all-to-all-start.3) | async-done | bytes 23068704 | tf_op jit(solution)/shard_map/all_to_all | solution.py:70
  359.4 29.0 %fusion.9 = f32[176,128,512]{2,1,0:T(8,128)} fusion(bf16[176,128,512]{2,1,0:T(8,128)(2,1)} %all-to-all-done.3, f32[176,128]{1,0:T(8,128)S(1)} %bitcast.53, s32[176,128]{1,0:T(8,128)S(1)} %add.223, f32[176,128]{1,0:T(8,128)S(1)} %bitcast.54, s32[176,128]{1,0:T(8,128)S(1)} %add.219, f32[176,128]{1,0:T(8,128)S(1)} %bitcast.55, s32[176,128]{1,0:T(8,128)S(1)} %add.215, ...), kind=kOutput, calls=%fused_computation.28 | convolution fusion | flops 3021996032 | bytes 70647808 | tf_op jit(solution)/shard_map/bcr,brf->bcf/dot_general | solution.py:76
  388.4 50.6 %fusion.35 = bf16[19,128,512]{2,0,1:T(8,128)(2,1)} fusion(f32[176,128,512]{2,1,0:T(8,128)} %fusion.9, s32[176]{0:T(256)S(1)} %broadcast_select_fusion), kind=kOutput, calls=%fused_computation.64 | convolution fusion | flops 2631077120 | bytes 48628416 | tf_op jit(solution)/shard_map/bs,bcf->scf/dot_general | solution.py:79
  439.0 3.6 copy.14
  442.6 5.2 slice_bitcast_fusion.3
  447.8 2.2 copy.15
  450.0 2.8 copy.16
  452.8 2.8 copy.17
  455.6 1.7 copy.18
  457.3 3.2 pad_maximum_fusion
  460.5 4.9 all-to-all-start.4
  465.4 4.6 convert_element_type.65
  470.0 19.1 %multiply_convert_fusion.1 = (bf16[1024,1024]{1,0:T(8,128)(2,1)}, bf16[1024,1024]{1,0:T(8,128)(2,1)}, bf16[1024,1024]{1,0:T(8,128)(2,1)}) fusion(f32[1024]{0:T(1024)S(1)} %subtract_multiply_fusion), kind=kLoop, calls=%fused_computation.50 | loop fusion | flops 22020096 | bytes 6295552 | tf_op jit(solution)/shard_map/convert.13
  489.1 30.1 %all-to-all-done.4 = bf16[4,19,32,2,256]{4,2,3,1,0:T(8,128)(2,1)S(1)} async-done(((bf16[4,19,32,2,256]{4,2,3,1,0:T(8,128)(2,1)}), bf16[4,19,32,2,256]{4,2,3,1,0:T(8,128)(2,1)S(1)}, u32[]{:S(2)}, u32[]{:S(2)}) %all-to-all-start.4) | async-done | bytes 2490400 | tf_op jit(solution)/shard_map/all_to_all | solution.py:83
  519.2 3.6 copy.19
  522.8 4.6 dot_general.13
  527.4 10.4 %fusion.53 = (bf16[19,32,2048]{2,1,0:T(8,128)(2,1)}, f32[19,32,2048]{2,1,0:T(8,128)S(1)}) fusion(bf16[19,32,2048]{2,1,0:T(8,128)(2,1)S(1)} %dot_general.13, bf16[1024,1024]{1,0:T(8,128)(2,1)} %get-tuple-element.24, bf16[1024,1024]{1,0:T(8,128)(2,1)} %get-tuple-element.23, bf16[1024,1024]{1,0:T(8,128)(2,1)} %get-tuple-element.22), kind=kOutput, calls=%fused_computation.109 | convolution fusion | flops 5135073280 | bytes 16252928 | tf_op jit(solution)/shard_map/dot_general | solution.py:89
  537.7 2.0 fusion.34
  539.8 34.8 %all-reduce.2.cloned.1.call-done = f32[19,1024]{1,0:T(8,128)} async-done(((f32[19,1024]{1,0:T(8,128)}), f32[19,1024]{1,0:T(8,128)}) %all-reduce.2.cloned.1.call-update) | async-done | bytes 77840 | tf_op jit(solution)/shard_map/psum | solution.py:94
  574.6 1.5 broadcast_multiply_fusion
  (34 shorter events, 0.3 us)
Async XLA Ops:
  7.2 9.6 %copy-start = (s32[12288]{0:T(1024)S(1)}, s32[12288]{0:T(1024)}, u32[]{:S(2)}) copy-start(s32[12288]{0:T(1024)} %param.8) | copy-start | bytes 147460
  11.6 9.8 %all-to-all-start = ((s32[8,22,1]{1,2,0:T(1,128)}), s32[8,22,1]{1,2,0:T(1,128)S(1)}, u32[]{:S(2)}, u32[]{:S(2)}) async-start(s32[8,22,1]{1,2,0:T(1,128)} %bitcast.2), calls=%async_computation | async-start | bytes 8192 | tf_op jit(solution)/shard_map/all_to_all | solution.py:71
  21.4 14.8 %all-to-all-start.1 = ((s32[8,22,128]{2,1,0:T(8,128)}), s32[8,22,128]{2,1,0:T(8,128)S(1)}, u32[]{:S(2)}, u32[]{:S(2)}) async-start(s32[8,22,128]{2,1,0:T(8,128)} %all_to_all.23), calls=%async_computation.1 | async-start | bytes 196608 | tf_op jit(solution)/shard_map/all_to_all | solution.py:72
  36.1 65.5 %all-to-all-start.2 = ((bf16[176,8,128]{2,1,0:T(8,128)(2,1)}), bf16[176,8,128]{2,1,0:T(8,128)(2,1)S(1)}, u32[]{:S(2)}, u32[]{:S(2)}) async-start(bf16[176,8,128]{2,1,0:T(8,128)(2,1)} %scatter_fusion), calls=%async_computation.2 | async-start | bytes 720896 | tf_op jit(solution)/shard_map/all_to_all | solution.py:73
  101.6 6.5 %copy-start.2 = (s32[80]{0:T(128)S(1)}, s32[80]{0:T(128)}, u32[]{:S(2)}) copy-start(s32[80]{0:T(128)} %param.12) | copy-start | bytes 964
  101.6 6.7 %copy-start.4 = (s32[8]{0:T(128)S(1)}, s32[8]{0:T(128)}, u32[]{:S(2)}) copy-start(s32[8]{0:T(128)} %param.10) | copy-start | bytes 100
  101.6 257.8 %all-to-all-start.3 = ((bf16[176,128,512]{2,1,0:T(8,128)(2,1)}), bf16[176,128,512]{2,1,0:T(8,128)(2,1)}, u32[]{:S(2)}, u32[]{:S(2)}) async-start(bf16[176,128,512]{2,1,0:T(8,128)(2,1)} %scatter_fusion.1), calls=%async_computation.3 | async-start | bytes 46137344 | tf_op jit(solution)/shard_map/all_to_all | solution.py:70
  447.8 7.8 %copy-start.3 = (bf16[1,19,32,2,256]{2,4,3,1,0:T(8,128)(2,1)S(1)}, bf16[1,19,32,2,256]{2,4,3,1,0:T(8,128)(2,1)}, u32[]{:S(2)}) copy-start(bf16[1,19,32,2,256]{2,4,3,1,0:T(8,128)(2,1)} %get-tuple-element.3) | copy-start | bytes 1867780
  460.5 58.7 %all-to-all-start.4 = ((bf16[4,19,32,2,256]{4,2,3,1,0:T(8,128)(2,1)}), bf16[4,19,32,2,256]{4,2,3,1,0:T(8,128)(2,1)S(1)}, u32[]{:S(2)}, u32[]{:S(2)}) async-start(bf16[4,19,32,2,256]{4,2,3,1,0:T(8,128)(2,1)} %pad_maximum_fusion), calls=%async_computation.4 | async-start | bytes 4980736 | tf_op jit(solution)/shard_map/all_to_all | solution.py:83
  465.4 109.2 %all-reduce.2.cloned.1.call-start = ((), (), s32[]{:S(2)}) async-start(), calls=%async_computation.5 | async-start | bytes 196608 | tf_op jit(solution)/shard_map/psum | solution.py:94
  522.8 15.0 %slice-start = ((s8[4980736]{0:T(1024)(128)(4,1)}), s8[786432]{0:T(1024)(128)(4,1)S(1)}, s32[]{:S(2)}) async-start(s8[4980736]{0:T(1024)(128)(4,1)} %bitcast.48), calls=%async_computation.6 | async-start | bytes 1572864
  527.4 10.4 %slice-start.1 = ((s8[4980736]{0:T(1024)(128)(4,1)}), s8[4194304]{0:T(1024)(128)(4,1)S(1)}, s32[]{:S(2)}) async-start(s8[4980736]{0:T(1024)(128)(4,1)} %bitcast.48), calls=%async_computation.7 | async-start | bytes 8388608
  537.7 38.4 %copy-start.1 = (s32[12288]{0:T(1024)S(1)}, s32[12288]{0:T(1024)}, u32[]{:S(2)}) copy-start(s32[12288]{0:T(1024)} %param.8) | copy-start | bytes 147460
Sparse Core Ops, SparseCore 0:
  539.9 34.6 all-reduce.1
